TPU v7x, 32 devices: a whole 2x2x4 slice. The times are simulated.
32 devices in a mesh: row: 4 (over y, x), col: 8 (over z, core).
Axes of the slice: x: 2, y: 2, z: 4, core: 2. Of those that a mesh axis runs over, the one named last changes fastest.
Arguments:
- covariance: float32 [20, 4, 10, 8, 256, 256], P(None, 'row', None, 'col'), may hold values from -0.006 to 2.4, as said below
- telemetry: bfloat16 [1536, 10, 8, 256], P('row', None, 'col'), may hold values from -6 to 6
- active: int32 [8, 1280], replicated, may hold values 0 or 1
- panel: int32 [1], replicated, may hold values from 0 to 75
Outputs:
- factored: float32 [20, 4, 10, 8, 256, 256], P(None, 'row', None, 'col')
Inputs may be any that keep to these rules, and one draw needn't show every extreme that they name: `covariance`: in every diagonal tile each diagonal entry exceeds the sum of magnitudes of the other entries of its row; entries off the matrix diagonal lie in -0.006 to 0.006.
All inputs are finite; a program needn't handle non-finite values.
Results may differ from a plain program's by a relative error of at most 0.0006.
Values may be sent and summed in bfloat16 or wider, within the bound.
No kernel may reach another device: no remote copies, remote signals or barrier semaphores. Data moves between devices by JAX's collectives and lax.ppermute only.
A program may use at most 384 MiB of HBM per device.

v0:
```python
import functools

import jax
import jax.numpy as jnp
from jax import lax
from jax.experimental import pallas as pl
from jax.experimental.pallas import tpu as pltpu
from jax.sharding import PartitionSpec as P


FORGET = 0.9
NT = (((1,), (1,)), ((), ()))


def from_root(block, axis, holder):
    block = jnp.where(lax.axis_index(axis) == holder, block, jnp.zeros_like(block))
    return lax.psum(block, axis)


def first_row(ids_ref, n_row, blocks_a):
    return jnp.minimum((ids_ref[2] - ids_ref[0] + n_row - 1) // n_row, blocks_a - 1)


def late_row(a, ids_ref, n_row, blocks_a):
    return jnp.maximum(a, first_row(ids_ref, n_row, blocks_a))


def refresh_kernel(ids_ref, row_ref, col_ref, c_ref, o_ref, *, n_row, n_col, blocks_b, samples):
    a = pl.program_id(0)
    r = ids_ref[0]
    c = ids_ref[1]
    k = ids_ref[2]
    i = a * n_row + r

    def one_tile(b, carry):
        j = b * n_col + c

        @pl.when((i >= j) & (j != k))
        def _():
            acc = None
            for d in range(n_row):
                part = lax.dot_general(
                    row_ref[0, d, 0], col_ref[ids_ref[3 + d], b], NT, preferred_element_type=jnp.float32
                )
                acc = part if acc is None else acc + part
            o_ref[0, 0, b, 0] = FORGET * c_ref[0, 0, b, 0] + acc / samples

        @pl.when((i < j) | (j == k))
        def _():
            o_ref[0, 0, b, 0] = c_ref[0, 0, b, 0]

        return carry

    lax.fori_loop(0, blocks_b, one_tile, 0)


def update_kernel(ids_ref, r_ref, prow_ref, pcol_ref, fac_ref, o_ref, *, n_row, n_col, blocks_a):
    start = first_row(ids_ref, n_row, blocks_a)
    a = late_row(pl.program_id(0), ids_ref, n_row, blocks_a)
    live = pl.program_id(0) >= start
    i = a * n_row + ids_ref[0]
    c = ids_ref[1]
    k = ids_ref[2]

    def one_tile(b, carry):
        j = b * n_col + c
        trailing = (i >= j) & (j > k)
        changed = trailing | ((j == k) & (i >= k))

        @pl.when(live & trailing)
        def _():
            upd = lax.dot_general(prow_ref[0], pcol_ref[b], NT, preferred_element_type=jnp.float32)
            o_ref[0, 0, b, 0] = r_ref[0, 0, b, 0] - upd

        @pl.when(live & (j == k) & (i > k))
        def _():
            o_ref[0, 0, b, 0] = prow_ref[0].astype(jnp.float32)

        @pl.when(live & (j == k) & (i == k))
        def _():
            o_ref[0, 0, b, 0] = fac_ref[...]

        @pl.when(live & jnp.logical_not(changed))
        def _():
            o_ref[0, 0, b, 0] = r_ref[0, 0, b, 0]

        return carry

    lax.fori_loop(0, pcol_ref.shape[0], one_tile, 0)


def gather_row(x, n_row):
    parts = [x]
    for s in range(1, n_row):
        parts.append(lax.ppermute(x, "row", [(q, (q + s) % n_row) for q in range(n_row)]))
    return jnp.stack(parts)


def body(covariance, telemetry, active, panel, *, n_row, n_col):
    return step(covariance, telemetry, active, panel, n_row=n_row, n_col=n_col)


def step(covariance, telemetry, active, panel, *, n_row, n_col):
    row_index = lax.axis_index("row")
    col_index = lax.axis_index("col")
    blocks_a = covariance.shape[0]
    blocks_b = covariance.shape[2]
    width = covariance.shape[4]
    ratio = n_col // n_row
    s_local = telemetry.shape[0]
    samples = s_local * n_row
    tiles = blocks_b * n_col
    prior = covariance[:, 0, :, 0]
    mask_full = jnp.concatenate([active, active], axis=1).reshape(tiles, width).astype(jnp.bfloat16)
    col_mask = lax.dynamic_index_in_dim(
        mask_full.reshape(blocks_b, n_col, width), col_index, 1, keepdims=False
    )
    local = telemetry[:, :, 0, :] * col_mask[None]
    local_t = jnp.transpose(local, (1, 2, 0))

    col_t = gather_row(local_t, n_row)
    mask = n_row - 2
    perm = []
    for src_r in range(n_row):
        for src_c in range(n_col):
            dst_r = src_c % n_row
            dst_c = (src_c // n_row) * n_row + (src_r ^ (dst_r & mask))
            perm.append((src_r * n_col + src_c, dst_r * n_col + dst_c))
    piece = lax.ppermute(local_t, ("row", "col"), perm)
    row_g = lax.all_gather(piece, "col", axis=0, tiled=False)
    row5 = row_g.reshape(ratio, n_row, blocks_b, width, s_local)
    quarter_of = jnp.bitwise_xor(jnp.arange(n_row, dtype=jnp.int32), row_index & mask)
    col_of = (row_index - quarter_of + n_row) % n_row

    panel_at = panel[0]
    owner_row = panel_at % n_row
    owner_col = panel_at % n_col
    ids = jnp.concatenate([jnp.stack([row_index, col_index, panel_at]), col_of]).astype(jnp.int32)

    own_diag = lax.dynamic_slice(
        prior, (panel_at // n_row, panel_at // n_col, 0, 0), (1, 1, width, width)
    )[0, 0]
    diag_prior = gather_row(own_diag, n_row)[(row_index - owner_row) % n_row]
    col_k = gather_row(lax.dynamic_index_in_dim(local_t, panel_at // n_col, 0, keepdims=False), n_row)
    gram_kk = jnp.einsum("pts,pus->tu", col_k, col_k, preferred_element_type=jnp.float32)
    diag_tile = FORGET * diag_prior + gram_kk / samples
    factor = jnp.linalg.cholesky(diag_tile)
    inverse = lax.linalg.triangular_solve(
        factor, jnp.eye(width, dtype=jnp.float32), left_side=True, lower=True
    )

    col_k_d = jnp.take(col_k, col_of, axis=0)
    gram_col = jnp.einsum(
        "hdbts,dus->bhtu", row5, col_k_d, preferred_element_type=jnp.float32
    ).reshape(blocks_a, width, width)
    prior_col = lax.dynamic_index_in_dim(prior, panel_at // n_col, 1, keepdims=False)
    column_part = FORGET * prior_col + gram_col / samples
    row_tiles = jnp.arange(blocks_a, dtype=jnp.int32) * n_row + row_index
    solved = jnp.einsum(
        "atu,vu->atv",
        column_part,
        inverse,
        precision=lax.Precision.HIGHEST,
        preferred_element_type=jnp.float32,
    )
    solved = jnp.where((row_tiles > panel_at)[:, None, None], solved, jnp.zeros_like(solved))
    panel_rows = from_root(solved.astype(jnp.bfloat16), "col", owner_col)
    pick = col_index // n_row
    chosen = lax.dynamic_index_in_dim(
        panel_rows.reshape(blocks_b, ratio, width, width), pick, 1, keepdims=False
    )
    received = None
    for s in range(1, n_row):
        pairs = []
        for cc in range(n_col):
            src_r = cc % n_row
            pairs.append((src_r * n_col + cc, ((src_r + s) % n_row) * n_col + cc))
        got = lax.ppermute(chosen, ("row", "col"), pairs)
        received = got if received is None else received + got
    panel_cols = jnp.where(row_index == col_index % n_row, chosen, received)

    full_row = (1, 1, blocks_b, 1, width, width)

    def late_pick(a, ids):
        return late_row(a, ids, n_row, blocks_a)

    refreshed = pl.pallas_call(
        functools.partial(
            refresh_kernel, n_row=n_row, n_col=n_col, blocks_b=blocks_b, samples=samples
        ),
        out_shape=jax.ShapeDtypeStruct(covariance.shape, jnp.float32),
        grid_spec=pltpu.PrefetchScalarGridSpec(
            num_scalar_prefetch=1,
            grid=(blocks_a,),
            in_specs=[
                pl.BlockSpec(
                    (1, n_row, 1, width, s_local),
                    lambda a, ids: (a % ratio, 0, a // ratio, 0, 0),
                ),
                pl.BlockSpec((n_row, blocks_b, width, s_local), lambda a, ids: (0, 0, 0, 0)),
                pl.BlockSpec(full_row, lambda a, ids: (a, 0, 0, 0, 0, 0)),
            ],
            out_specs=pl.BlockSpec(full_row, lambda a, ids: (a, 0, 0, 0, 0, 0)),
        ),
        compiler_params=pltpu.CompilerParams(vmem_limit_bytes=48 * 1024 * 1024),
    )(ids, row5, col_t, covariance)

    result = pl.pallas_call(
        functools.partial(update_kernel, n_row=n_row, n_col=n_col, blocks_a=blocks_a),
        out_shape=jax.ShapeDtypeStruct(covariance.shape, jnp.float32),
        grid_spec=pltpu.PrefetchScalarGridSpec(
            num_scalar_prefetch=1,
            grid=(blocks_a,),
            in_specs=[
                pl.BlockSpec(full_row, lambda a, ids: (late_pick(a, ids), 0, 0, 0, 0, 0)),
                pl.BlockSpec((1, width, width), lambda a, ids: (late_pick(a, ids), 0, 0)),
                pl.BlockSpec((blocks_b, width, width), lambda a, ids: (0, 0, 0)),
                pl.BlockSpec((width, width), lambda a, ids: (0, 0)),
            ],
            out_specs=pl.BlockSpec(full_row, lambda a, ids: (late_pick(a, ids), 0, 0, 0, 0, 0)),
        ),
        input_output_aliases={1: 0},
        compiler_params=pltpu.CompilerParams(vmem_limit_bytes=48 * 1024 * 1024),
    )(ids, refreshed, panel_rows, panel_cols, factor)
    return result


def solution(mesh):
    n_row = mesh.shape["row"]
    n_col = mesh.shape["col"]
    in_specs = (P(None, "row", None, "col", None, None), P("row", None, "col", None), P(), P())
    out_specs = P(None, "row", None, "col", None, None)
    return jax.shard_map(
        functools.partial(body, n_row=n_row, n_col=n_col),
        mesh=mesh,
        in_specs=in_specs,
        out_specs=out_specs,
        check_vma=False,
    )
```

profile of v0, /device:TPU:0, one launch (start us, length us, event | category | flops | bytes accessed | tf_op | source)
XLA Modules:
  0.0 423.7 jit_solution(7973907222820443895)
XLA Ops:
  7.4 2.8 copy.31
  10.7 1.3 copy-done.1
  12.0 1.9 collective-permute-start
  15.8 49.7 %collective-permute-start.9 = (f32[256,256]{0,1:T(8,128)S(1)}, f32[256,256]{0,1:T(8,128)}, u32[]{:S(2)}, u32[]{:S(2)}) collective-permute-start(f32[256,256]{0,1:T(8,128)S(1)} %bitcast.131), channel_id=1, source_target_pairs={{0,24},{8,0},{16,8},{24,16},{1,25},{9,1},{17,9},{25,17},{2,26},{10... | collective-permute-start | bytes 786440 | tf_op jit(solution)/shard_map/ppermute | solution.py:95
  66.7 2.2 collective-permute-start.6
  69.0 2.0 collective-permute-start.5
  71.0 8.4 %collective-permute-done.6 = bf16[256,384]{1,0:T(8,128)(2,1)S(1)} collective-permute-done((bf16[256,384]{1,0:T(8,128)(2,1)S(1)}, bf16[256,384]{1,0:T(8,128)(2,1)S(1)}, u32[]{:S(2)}, u32[]{:S(2)}) %collective-permute-start.6) | collective-permute-done | bytes 196640 | tf_op jit(solution)/shard_map/ppermute | solution.py:95
  79.5 2.7 collective-permute-start.4
  82.2 1.4 collective-permute-start.2
  83.6 3.1 collective-permute-done.4
  86.7 1.7 collective-permute-start.1
  89.5 1.6 gather_fusion
  92.3 1.8 fusion.11
  94.3 11.7 %cholesky.50 = f32[128,128]{1,0:T(8,128)S(1)} custom-call(f32[128,128]{1,0:T(8,128)S(1)} %cholesky.118), custom_call_target="Cholesky" | custom-call | tf_op jit(solution)/shard_map/jit(cholesky)/cholesky | solution.py:147
  106.0 9.8 %custom-call.14 = f32[1,128,128]{1,2,0:T(8,128)S(1)} custom-call(f32[1,128,128]{2,1,0:T(8,128)S(1)} %get-tuple-element.32), custom_call_target="InvertDiagBlocksLowerTriangular" | custom-call | tf_op jit(solution)/shard_map/jit(cholesky)/cholesky | solution.py:147
  116.4 11.7 %cholesky.105 = f32[128,128]{1,0:T(8,128)S(1)} custom-call(f32[128,128]{1,0:T(8,128)S(1)} %convolution_subtract_fusion.1), custom_call_target="Cholesky" | custom-call | tf_op jit(solution)/shard_map/jit(cholesky)/cholesky | solution.py:147
  130.1 5.2 %while.1 = (s32[]{:T(128)}, f32[256,256]{1,0:T(8,128)S(1)}, s32[2,2]{1,0:T(2,128)S(1)}, f32[2,128,128]{2,1,0:T(8,128)}, s32[]{:T(128)}) while((s32[]{:T(128)}, f32[256,256]{1,0:T(8,128)S(1)}, s32[2,2]{1,0:T(2,128)S(1)}, f32[2,128,128]{2,1,0:T(8,128)}, s32[]{:T(128)}) %tuple.26), condition=%wide.while_cond, body=%wide.while_body.sunk | while | flops 2 | bytes 132205 | solution.py:148
  130.8 1.9 bitcast_dynamic-update-slice_fusion.2
  133.3 1.9 bitcast_dynamic-update-slice_fusion.2
  135.3 20.5 %custom-call.15 = f32[2,128,128]{1,2,0:T(8,128)S(1)} custom-call(f32[2,128,128]{2,1,0:T(8,128)} %get-tuple-element.12), custom_call_target="InvertDiagBlocksLowerTriangular" | custom-call | tf_op jit(solution)/shard_map/triangular_solve | solution.py:148
  156.6 48.4 %all-gather.3.cloned.1.call-done = bf16[80,256,384]{2,1,0:T(8,128)(2,1)} async-done(((bf16[10,256,384]{2,1,0:T(8,128)(2,1)}), bf16[80,256,384]{2,1,0:T(8,128)(2,1)}) %all-gather.3.cloned.1.call-update) | async-done | bytes 15728656 | tf_op jit(solution)/shard_map/all_gather | solution.py:130
  205.0 12.4 %fusion = f32[10,2,256,256]{2,3,0,1:T(8,128)} fusion(bf16[2,4,10,256,384]{4,3,2,1,0:T(8,128)(2,1)} %bitcast.129, bf16[4,256,384]{2,1,0:T(8,128)(2,1)} %gather_fusion, pred[4]{0:T(512)(128)(4,1)S(1)} %get-tuple-element.23), kind=kOutput, calls=%fused_computation.5 | convolution fusion | flops 4028235776 | bytes 21757956 | tf_op jit(solution)/shard_map/hdbts,dus->bhtu/dot_general | solution.py:153
  217.3 5.9 %copy.34 = f32[10,2,256,256]{3,2,1,0:T(8,128)} copy(f32[10,2,256,256]{2,3,0,1:T(8,128)} %fusion) | data formatting | bytes 10485760 | tf_op jit(solution)/shard_map/div | solution.py:157
  223.2 9.9 %fusion.6 = bf16[20,256,256]{2,1,0:T(8,128)(2,1)} fusion(pred[20]{0:T(512)(128)(4,1)S(1)} %add_compare_fusion, pred[]{:T(512)S(6)} %eq.18, f32[20,256,256]{2,1,0:T(8,128)} %bitcast.128, f32[20,1,10,1,256,256]{5,4,3,2,1,0:T(8,128)} %c_ref.1, s32[]{:T(128)S(6)} %select_n.118, f32[128,256]{1,0:T(8,128)S(1)} %fusion.28, f32[128,256]{1,0:T(8,128)S(1)} %fusion.25), kind=kOutput, calls=%fused_computation.12 | convolution fusion | flops 4033150976 | bytes 13369369 | tf_op jit(solution)/shard_map/atu,vu->atv/dot_general | solution.py:159
  233.2 67.4 %all-reduce.3.cloned.1.call-done.prow_ref = bf16[20,256,256]{2,1,0:T(8,128)(2,1)} async-done(((bf16[20,256,256]{2,1,0:T(8,128)(2,1)}), bf16[20,256,256]{2,1,0:T(8,128)(2,1)}) %all-reduce.3.cloned.1.call-update) | async-done | bytes 2621456 | tf_op jit(solution)/shard_map/psum | solution.py:17
  300.6 1.4 dynamic-slice_bitcast_fusion
  302.0 4.4 %collective-permute-start.12 = (bf16[10,256,256]{2,1,0:T(8,128)(2,1)S(1)}, bf16[10,256,256]{2,1,0:T(8,128)(2,1)S(1)}, u32[]{:S(2)}, u32[]{:S(2)}) collective-permute-start(bf16[10,256,256]{2,1,0:T(8,128)(2,1)S(1)} %dynamic-slice_bitcast_fusion), channel_id=1, source_target_pairs={{0,24},{9,1},{18,10},{27,19},{4,28},{13,5},{22,14},{31,23}} | collective-permute-start | bytes 3932168 | tf_op jit(solution)/shard_map/ppermute | solution.py:178
  306.4 1.4 collective-permute-start.11
  307.8 1.4 collective-permute-start.10
  309.6 6.5 %pad_maximum_fusion.col_ref = bf16[4,10,256,384]{3,2,1,0:T(8,128)(2,1)} fusion(bf16[1,10,256,384]{3,2,1,0:T(8,128)(2,1)} %bitcast.8, bf16[1,10,256,384]{3,2,1,0:T(8,128)(2,1)} %bitcast.7, bf16[1,10,256,384]{3,2,1,0:T(8,128)(2,1)} %bitcast.6, bf16[1,10,256,384]{3,2,1,0:T(8,128)(2,1)S(1)} %fusion.45), kind=kLoop, calls=%fused_computation.3 | loop fusion | flops 11796480 | bytes 15728640 | tf_op jit(solution)/shard_map/stack | solution.py:96
  316.1 70.1 %shard_map.46.r_ref = f32[20,1,10,1,256,256]{5,4,3,2,1,0:T(8,128)} custom-call(s32[7]{0:T(128)S(1)} %pad_add_fusion.ids_ref, bf16[2,4,10,256,384]{4,3,2,1,0:T(8,128)(2,1)} %bitcast.130, bf16[4,10,256,384]{3,2,1,0:T(8,128)(2,1)} %pad_maximum_fusion.col_ref, f32[20,1,10,1,256,256]{5,4,3,2,1,0:T(8,128)} %c_ref.1), custom_call_target="tpu_custom_call" | custom-call | tf_op jit(solution)/shard_map/pallas_call | solution.py:187
  386.5 30.3 %shard_map.47 = f32[20,1,10,1,256,256]{5,4,3,2,1,0:T(8,128)} custom-call(s32[7]{0:T(128)S(1)} %pad_add_fusion.ids_ref, f32[20,1,10,1,256,256]{5,4,3,2,1,0:T(8,128)} %shard_map.46.r_ref, bf16[20,256,256]{2,1,0:T(8,128)(2,1)S(1)} %copy-done, bf16[10,256,256]{2,1,0:T(8,128)(2,1)S(1)} %add_select_fusion.pcol_ref, ...), custom_call_target="tpu_custom_call", output_to_operand_aliasing={{}: (1, {})} | custom-call | tf_op jit(solution)/shard_map/pallas_call | solution.py:208
  (64 shorter events, 10.4 us)
Async XLA Ops:
  6.5 198.5 %all-gather.3.cloned.1.call-start = ((), (), s32[]{:S(2)}) async-start(), calls=%async_computation.1 | async-start | bytes 17694720 | tf_op jit(solution)/shard_map/all_gather | solution.py:130
  10.7 1.3 copy-start.1
  12.0 1.9 collective-permute-start
  14.0 286.7 %all-reduce.3.cloned.1.call-start = ((), (), s32[]{:S(2)}) async-start(), calls=%async_computation | async-start | bytes 5242880 | tf_op jit(solution)/shard_map/psum | solution.py:17
  15.8 75.3 %collective-permute-start.9 = (f32[256,256]{0,1:T(8,128)S(1)}, f32[256,256]{0,1:T(8,128)}, u32[]{:S(2)}, u32[]{:S(2)}) collective-permute-start(f32[256,256]{0,1:T(8,128)S(1)} %bitcast.131), channel_id=1, source_target_pairs={{0,24},{8,0},{16,8},{24,16},{1,25},{9,1},{17,9},{25,17},{2,26},{10... | collective-permute-start | bytes 786440 | tf_op jit(solution)/shard_map/ppermute | solution.py:95
  65.5 26.8 %collective-permute-start.8 = (f32[256,256]{0,1:T(8,128)S(1)}, f32[256,256]{0,1:T(8,128)}, u32[]{:S(2)}, u32[]{:S(2)}) collective-permute-start(f32[256,256]{0,1:T(8,128)S(1)} %bitcast.132), channel_id=1, source_target_pairs={{0,16},{8,24},{16,0},{24,8},{1,17},{9,25},{17,1},{25,9},{2,18},{10... | collective-permute-start | bytes 786440 | tf_op jit(solution)/shard_map/ppermute | solution.py:95
  65.5 26.8 %collective-permute-start.7 = (f32[256,256]{0,1:T(8,128)S(1)}, f32[256,256]{0,1:T(8,128)}, u32[]{:S(2)}, u32[]{:S(2)}) collective-permute-start(f32[256,256]{0,1:T(8,128)S(1)} %bitcast.133), channel_id=1, source_target_pairs={{0,8},{8,16},{16,24},{24,0},{1,9},{9,17},{17,25},{25,1},{2,10},{10... | collective-permute-start | bytes 786440 | tf_op jit(solution)/shard_map/ppermute | solution.py:95
  66.7 12.7 %collective-permute-start.6 = (bf16[256,384]{1,0:T(8,128)(2,1)S(1)}, bf16[256,384]{1,0:T(8,128)(2,1)S(1)}, u32[]{:S(2)}, u32[]{:S(2)}) collective-permute-start(bf16[256,384]{1,0:T(8,128)(2,1)S(1)} %get-tuple-element.28), channel_id=1, source_target_pairs={{0,24},{8,0},{16,8},{24,16},{1,25},{9,1},{17,9},{25,17},{2,26},{10... | collective-permute-start | bytes 589832 | tf_op jit(solution)/shard_map/ppermute | solution.py:95
  69.0 13.2 %collective-permute-start.5 = (bf16[256,384]{1,0:T(8,128)(2,1)S(1)}, bf16[256,384]{1,0:T(8,128)(2,1)S(1)}, u32[]{:S(2)}, u32[]{:S(2)}) collective-permute-start(bf16[256,384]{1,0:T(8,128)(2,1)S(1)} %get-tuple-element.28), channel_id=1, source_target_pairs={{0,16},{8,24},{16,0},{24,8},{1,17},{9,25},{17,1},{25,9},{2,18},{10... | collective-permute-start | bytes 589832 | tf_op jit(solution)/shard_map/ppermute | solution.py:95
  79.5 7.2 %collective-permute-start.4 = (bf16[256,384]{1,0:T(8,128)(2,1)S(1)}, bf16[256,384]{1,0:T(8,128)(2,1)S(1)}, u32[]{:S(2)}, u32[]{:S(2)}) collective-permute-start(bf16[256,384]{1,0:T(8,128)(2,1)S(1)} %get-tuple-element.28), channel_id=1, source_target_pairs={{0,8},{8,16},{16,24},{24,0},{1,9},{9,17},{17,25},{25,1},{2,10},{10... | collective-permute-start | bytes 589832 | tf_op jit(solution)/shard_map/ppermute | solution.py:95
  82.2 6.2 %copy-start.2 = (bf16[256,384]{1,0:T(8,128)(2,1)}, bf16[256,384]{1,0:T(8,128)(2,1)S(1)}, u32[]{:S(2)}) copy-start(bf16[256,384]{1,0:T(8,128)(2,1)S(1)} %collective-permute-done.5) | copy-start | bytes 589828
  82.2 225.6 %collective-permute-start.2 = (bf16[10,256,384]{2,1,0:T(8,128)(2,1)}, bf16[10,256,384]{2,1,0:T(8,128)(2,1)}, u32[]{:S(2)}, u32[]{:S(2)}) collective-permute-start(bf16[10,256,384]{2,1,0:T(8,128)(2,1)} %copy-done.1), channel_id=1, source_target_pairs={{0,16},{8,24},{16,0},{24,8},{1,17},{9,25},{17,1},{25,9},{2,18},{10... | collective-permute-start | bytes 5898248 | tf_op jit(solution)/shard_map/ppermute | solution.py:95
  86.6 1.7 copy-start.3
  86.7 223.0 %collective-permute-start.1 = (bf16[10,256,384]{2,1,0:T(8,128)(2,1)}, bf16[10,256,384]{2,1,0:T(8,128)(2,1)}, u32[]{:S(2)}, u32[]{:S(2)}) collective-permute-start(bf16[10,256,384]{2,1,0:T(8,128)(2,1)} %copy-done.1), channel_id=1, source_target_pairs={{0,8},{8,16},{16,24},{24,0},{1,9},{9,17},{17,25},{25,1},{2,10},{10... | collective-permute-start | bytes 5898248 | tf_op jit(solution)/shard_map/ppermute | solution.py:95
  91.1 218.5 %collective-permute-start.3 = (bf16[10,256,384]{2,1,0:T(8,128)(2,1)}, bf16[10,256,384]{2,1,0:T(8,128)(2,1)}, u32[]{:S(2)}, u32[]{:S(2)}) collective-permute-start(bf16[10,256,384]{2,1,0:T(8,128)(2,1)} %copy-done.1), channel_id=1, source_target_pairs={{0,24},{8,0},{16,8},{24,16},{1,25},{9,1},{17,9},{25,17},{2,26},{10... | collective-permute-start | bytes 5898248 | tf_op jit(solution)/shard_map/ppermute | solution.py:95
  302.0 84.2 %collective-permute-start.12 = (bf16[10,256,256]{2,1,0:T(8,128)(2,1)S(1)}, bf16[10,256,256]{2,1,0:T(8,128)(2,1)S(1)}, u32[]{:S(2)}, u32[]{:S(2)}) collective-permute-start(bf16[10,256,256]{2,1,0:T(8,128)(2,1)S(1)} %dynamic-slice_bitcast_fusion), channel_id=1, source_target_pairs={{0,24},{9,1},{18,10},{27,19},{4,28},{13,5},{22,14},{31,23}} | collective-permute-start | bytes 3932168 | tf_op jit(solution)/shard_map/ppermute | solution.py:178
  306.4 79.9 %collective-permute-start.11 = (bf16[10,256,256]{2,1,0:T(8,128)(2,1)S(1)}, bf16[10,256,256]{2,1,0:T(8,128)(2,1)S(1)}, u32[]{:S(2)}, u32[]{:S(2)}) collective-permute-start(bf16[10,256,256]{2,1,0:T(8,128)(2,1)S(1)} %dynamic-slice_bitcast_fusion), channel_id=1, source_target_pairs={{0,16},{9,25},{18,2},{27,11},{4,20},{13,29},{22,6},{31,15}} | collective-permute-start | bytes 3932168 | tf_op jit(solution)/shard_map/ppermute | solution.py:178
  307.8 78.5 %collective-permute-start.10 = (bf16[10,256,256]{2,1,0:T(8,128)(2,1)S(1)}, bf16[10,256,256]{2,1,0:T(8,128)(2,1)S(1)}, u32[]{:S(2)}, u32[]{:S(2)}) collective-permute-start(bf16[10,256,256]{2,1,0:T(8,128)(2,1)S(1)} %dynamic-slice_bitcast_fusion), channel_id=1, source_target_pairs={{0,8},{9,17},{18,26},{27,3},{4,12},{13,21},{22,30},{31,7}} | collective-permute-start | bytes 3932168 | tf_op jit(solution)/shard_map/ppermute | solution.py:178
  316.1 70.2 %copy-start = (bf16[20,256,256]{2,1,0:T(8,128)(2,1)S(1)}, bf16[20,256,256]{2,1,0:T(8,128)(2,1)}, u32[]{:S(2)}) copy-start(bf16[20,256,256]{2,1,0:T(8,128)(2,1)} %all-reduce.3.cloned.1.call-done.prow_ref) | copy-start | bytes 7864324
Sparse Core Ops, SparseCore 0:
  14.1 190.8 all-gather.2
  233.3 67.3 all-reduce.2
where the time goes:
time: 425 us; the launch traced here: 424 us
  waiting for transfers between devices  127 us (30%)
  Pallas kernels  100 us (24%)
  starting transfers between devices  70.8 us (17%)
  other arithmetic  64.6 us (15%)
  matrix products  25.3 us (6%)
  local copies, waits for them, and re-layouts  19.5 us (5%)
  between operations  15.6 us (4%)
    pallas_call x1, Pallas kernels, step(): pl.pallas_call(functools.partial(refresh_kernel, n_row=n_row, n_col=n_col...  70.1 us
    psum x1, waiting for transfers between devices, from_root(): return lax.psum(block, axis)  67.4 us
    ppermute x9, starting transfers between devices, gather_row(): lax.ppermute(x, 'row', [(q, (q + s) % n_row) for q in range(n_row)])  61.7 us
    all_gather x1, waiting for transfers between devices, step(): row_g = lax.all_gather(piece, 'col', axis=0, tiled=False)  48.4 us
    another operation x6, other arithmetic, step(): factor = jnp.linalg.cholesky(diag_tile)  33.9 us
    pallas_call x1, Pallas kernels, step(): pl.pallas_call(functools.partial(update_kernel, n_row=n_row, n_col=n_col,...  30.3 us
    another operation x3, other arithmetic, step(): lax.linalg.triangular_solve(factor, jnp.eye(width, dtype=jnp.float32), le...  20.5 us
    dot_general x1, matrix products, step(): jnp.einsum('hdbts,dus->bhtu', row5, col_k_d, preferred_element_type=jnp.f...  12.4 us
  transfers between devices with their start and end apart: 15, of which 4 were waited for; matrix products, arithmetic and copies ran while one was open for 24% of the time, Pallas kernels for 17%

commit v1 on v0

--- a/solution.py
+++ b/solution.py
@@ -25,8 +25,9 @@
     return jnp.maximum(a, first_row(ids_ref, n_row, blocks_a))
 
 
-def refresh_kernel(ids_ref, row_ref, col_ref, c_ref, o_ref, *, n_row, n_col, blocks_b, samples):
-    a = pl.program_id(0)
+def refresh_kernel(ids_ref, row_ref, col_ref, c_ref, *refs, n_row, n_col, blocks_b, samples, offset):
+    o_ref = refs[-1]
+    a = pl.program_id(0) + offset
     r = ids_ref[0]
     c = ids_ref[1]
     k = ids_ref[2]
@@ -184,26 +185,35 @@
     def late_pick(a, ids):
         return late_row(a, ids, n_row, blocks_a)
 
-    refreshed = pl.pallas_call(
-        functools.partial(
-            refresh_kernel, n_row=n_row, n_col=n_col, blocks_b=blocks_b, samples=samples
-        ),
-        out_shape=jax.ShapeDtypeStruct(covariance.shape, jnp.float32),
-        grid_spec=pltpu.PrefetchScalarGridSpec(
-            num_scalar_prefetch=1,
-            grid=(blocks_a,),
-            in_specs=[
-                pl.BlockSpec(
-                    (1, n_row, 1, width, s_local),
-                    lambda a, ids: (a % ratio, 0, a // ratio, 0, 0),
-                ),
-                pl.BlockSpec((n_row, blocks_b, width, s_local), lambda a, ids: (0, 0, 0, 0)),
-                pl.BlockSpec(full_row, lambda a, ids: (a, 0, 0, 0, 0, 0)),
-            ],
-            out_specs=pl.BlockSpec(full_row, lambda a, ids: (a, 0, 0, 0, 0, 0)),
-        ),
-        compiler_params=pltpu.CompilerParams(vmem_limit_bytes=48 * 1024 * 1024),
-    )(ids, row5, col_t, covariance)
+    half = blocks_a // 2
+
+    def refresh_half(offset, rows, prev):
+        extra = [] if prev is None else [prev]
+        return pl.pallas_call(
+            functools.partial(
+                refresh_kernel, n_row=n_row, n_col=n_col, blocks_b=blocks_b, samples=samples,
+                offset=offset,
+            ),
+            out_shape=jax.ShapeDtypeStruct(covariance.shape, jnp.float32),
+            grid_spec=pltpu.PrefetchScalarGridSpec(
+                num_scalar_prefetch=1,
+                grid=(rows,),
+                in_specs=[
+                    pl.BlockSpec(
+                        (1, n_row, 1, width, s_local),
+                        lambda a, ids: ((a + offset) % ratio, 0, (a + offset) // ratio, 0, 0),
+                    ),
+                    pl.BlockSpec((n_row, blocks_b, width, s_local), lambda a, ids: (0, 0, 0, 0)),
+                    pl.BlockSpec(full_row, lambda a, ids: (a + offset, 0, 0, 0, 0, 0)),
+                ] + [pl.BlockSpec(memory_space=pl.ANY)] * len(extra),
+                out_specs=pl.BlockSpec(full_row, lambda a, ids: (a + offset, 0, 0, 0, 0, 0)),
+            ),
+            input_output_aliases={} if prev is None else {4: 0},
+            compiler_params=pltpu.CompilerParams(vmem_limit_bytes=48 * 1024 * 1024),
+        )(ids, row5, col_t, covariance, *extra)
+
+    refreshed = refresh_half(0, half, None)
+    refreshed = refresh_half(half, blocks_a - half, refreshed)
 
     result = pl.pallas_call(
         functools.partial(update_kernel, n_row=n_row, n_col=n_col, blocks_a=blocks_a),

time: 425 us -> 431 us (1.014)
  Pallas kernels: 100 us -> 106 us
    pallas_call x1 -> x2, Pallas kernels: 70.1 us -> 76.1 us  [refresh_half(): pl.pallas_call(functools.partial(refresh_kernel, n_row=n_row, n_col=n_col...]
  transfers between devices with their start and end apart: 15 -> 15, of which waited for: 4 -> 5; matrix products, arithmetic and copies ran while one was open for 24% -> 24% of each run, Pallas kernels for 17% -> 18%
where the time goes in v1:
time: 431 us; the launch traced here: 430 us
  waiting for transfers between devices  129 us (30%)
  Pallas kernels  106 us (25%)
  starting transfers between devices  67.9 us (16%)
  other arithmetic  64.6 us (15%)
  matrix products  25.3 us (6%)
  local copies, waits for them, and re-layouts  20.6 us (5%)
  between operations  15.7 us (4%)
    pallas_call x2, Pallas kernels, refresh_half(): pl.pallas_call(functools.partial(refresh_kernel, n_row=n_row, n_col=n_col...  76.1 us
    psum x1, waiting for transfers between devices, from_root(): return lax.psum(block, axis)  67.4 us
    ppermute x9, starting transfers between devices, gather_row(): lax.ppermute(x, 'row', [(q, (q + s) % n_row) for q in range(n_row)])  58.9 us
    all_gather x1, waiting for transfers between devices, step(): row_g = lax.all_gather(piece, 'col', axis=0, tiled=False)  51.9 us
    another operation x6, other arithmetic, step(): factor = jnp.linalg.cholesky(diag_tile)  34 us
    pallas_call x1, Pallas kernels, step(): pl.pallas_call(functools.partial(update_kernel, n_row=n_row, n_col=n_col,...  30.3 us
    another operation x3, other arithmetic, step(): lax.linalg.triangular_solve(factor, jnp.eye(width, dtype=jnp.float32), le...  20.5 us
    dot_general x1, matrix products, step(): jnp.einsum('hdbts,dus->bhtu', row5, col_k_d, preferred_element_type=jnp.f...  12.4 us
  transfers between devices with their start and end apart: 15, of which 5 were waited for; matrix products, arithmetic and copies ran while one was open for 24% of the time, Pallas kernels for 18%

profile of v1, /device:TPU:0, one launch (start us, length us, event | category | flops | bytes accessed | tf_op | source)
XLA Modules:
  0.0 429.6 jit_solution(9337515854201796425)
XLA Ops:
  7.4 2.8 copy.32
  10.7 1.3 copy-done.1
  12.0 1.9 collective-permute-start
  15.8 49.7 %collective-permute-start.6 = (bf16[256,384]{1,0:T(8,128)(2,1)}, bf16[256,384]{1,0:T(8,128)(2,1)S(1)}, u32[]{:S(2)}, u32[]{:S(2)}) collective-permute-start(bf16[256,384]{1,0:T(8,128)(2,1)} %get-tuple-element.28), channel_id=1, source_target_pairs={{0,24},{8,0},{16,8},{24,16},{1,25},{9,1},{17,9},{25,17},{2,26},{10... | collective-permute-start | bytes 589832 | tf_op jit(solution)/shard_map/ppermute | solution.py:96
  66.2 1.0 constant_dynamic-slice_fusion.1
  67.3 2.8 collective-permute-start.7
  71.1 3.3 collective-permute-start.9
  74.4 8.4 %collective-permute-done.5 = bf16[256,384]{1,0:T(8,128)(2,1)S(1)} collective-permute-done((bf16[256,384]{1,0:T(8,128)(2,1)}, bf16[256,384]{1,0:T(8,128)(2,1)S(1)}, u32[]{:S(2)}, u32[]{:S(2)}) %collective-permute-start.5) | collective-permute-done | bytes 196640 | tf_op jit(solution)/shard_map/ppermute | solution.py:96
  83.5 1.1 pad_maximum_fusion.1
  84.6 1.6 gather_fusion
  86.2 2.0 collective-permute-start.1
  88.5 1.8 fusion.11
  90.4 11.7 %cholesky.50 = f32[128,128]{1,0:T(8,128)S(1)} custom-call(f32[128,128]{1,0:T(8,128)S(1)} %cholesky.118), custom_call_target="Cholesky" | custom-call | tf_op jit(solution)/shard_map/jit(cholesky)/cholesky | solution.py:148
  102.2 9.8 %custom-call.14 = f32[1,128,128]{1,2,0:T(8,128)S(1)} custom-call(f32[1,128,128]{2,1,0:T(8,128)S(1)} %get-tuple-element.32), custom_call_target="InvertDiagBlocksLowerTriangular" | custom-call | tf_op jit(solution)/shard_map/jit(cholesky)/cholesky | solution.py:148
  112.5 11.7 %cholesky.105 = f32[128,128]{1,0:T(8,128)S(1)} custom-call(f32[128,128]{1,0:T(8,128)S(1)} %convolution_subtract_fusion.1), custom_call_target="Cholesky" | custom-call | tf_op jit(solution)/shard_map/jit(cholesky)/cholesky | solution.py:148
  126.4 5.3 %while.1 = (s32[]{:T(128)}, f32[256,256]{1,0:T(8,128)S(1)}, s32[2,2]{1,0:T(2,128)S(1)}, f32[2,128,128]{2,1,0:T(8,128)}, s32[]{:T(128)}) while((s32[]{:T(128)}, f32[256,256]{1,0:T(8,128)S(1)}, s32[2,2]{1,0:T(2,128)S(1)}, f32[2,128,128]{2,1,0:T(8,128)}, s32[]{:T(128)}) %tuple.26), condition=%wide.while_cond, body=%wide.while_body.sunk | while | flops 2 | bytes 132205 | solution.py:149
  127.1 2.0 bitcast_dynamic-update-slice_fusion.2
  129.7 2.0 bitcast_dynamic-update-slice_fusion.2
  131.7 20.5 %custom-call.15 = f32[2,128,128]{1,2,0:T(8,128)S(1)} custom-call(f32[2,128,128]{2,1,0:T(8,128)} %get-tuple-element.12), custom_call_target="InvertDiagBlocksLowerTriangular" | custom-call | tf_op jit(solution)/shard_map/triangular_solve | solution.py:149
  153.1 51.9 %all-gather.3.cloned.1.call-done = bf16[80,256,384]{2,1,0:T(8,128)(2,1)} async-done(((bf16[10,256,384]{2,1,0:T(8,128)(2,1)}), bf16[80,256,384]{2,1,0:T(8,128)(2,1)}) %all-gather.3.cloned.1.call-update) | async-done | bytes 15728656 | tf_op jit(solution)/shard_map/all_gather | solution.py:131
  205.0 12.4 %fusion = f32[10,2,256,256]{2,3,0,1:T(8,128)} fusion(bf16[2,4,10,256,384]{4,3,2,1,0:T(8,128)(2,1)} %bitcast.128, bf16[4,256,384]{2,1,0:T(8,128)(2,1)} %gather_fusion, pred[4]{0:T(512)(128)(4,1)S(1)} %get-tuple-element.23), kind=kOutput, calls=%fused_computation.5 | convolution fusion | flops 4028235776 | bytes 21757956 | tf_op jit(solution)/shard_map/hdbts,dus->bhtu/dot_general | solution.py:154
  217.3 5.9 %copy.35 = f32[10,2,256,256]{3,2,1,0:T(8,128)} copy(f32[10,2,256,256]{2,3,0,1:T(8,128)} %fusion) | data formatting | bytes 10485760 | tf_op jit(solution)/shard_map/div | solution.py:158
  223.2 9.9 %fusion.6 = bf16[20,256,256]{2,1,0:T(8,128)(2,1)} fusion(pred[20]{0:T(512)(128)(4,1)S(1)} %add_compare_fusion, pred[]{:T(512)S(6)} %eq.18, f32[20,256,256]{2,1,0:T(8,128)} %bitcast.131, f32[20,1,10,1,256,256]{5,4,3,2,1,0:T(8,128)} %c_ref.3, s32[]{:T(128)S(6)} %select_n.118, f32[128,256]{1,0:T(8,128)S(1)} %fusion.28, f32[128,256]{1,0:T(8,128)S(1)} %fusion.25), kind=kOutput, calls=%fused_computation.12 | convolution fusion | flops 4033150976 | bytes 13369369 | tf_op jit(solution)/shard_map/atu,vu->atv/dot_general | solution.py:160
  233.2 67.4 %all-reduce.3.cloned.1.call-done.prow_ref = bf16[20,256,256]{2,1,0:T(8,128)(2,1)} async-done(((bf16[20,256,256]{2,1,0:T(8,128)(2,1)}), bf16[20,256,256]{2,1,0:T(8,128)(2,1)}) %all-reduce.3.cloned.1.call-update) | async-done | bytes 2621456 | tf_op jit(solution)/shard_map/psum | solution.py:17
  300.6 1.4 dynamic-slice_bitcast_fusion
  302.0 4.4 %collective-permute-start.12 = (bf16[10,256,256]{2,1,0:T(8,128)(2,1)S(1)}, bf16[10,256,256]{2,1,0:T(8,128)(2,1)S(1)}, u32[]{:S(2)}, u32[]{:S(2)}) collective-permute-start(bf16[10,256,256]{2,1,0:T(8,128)(2,1)S(1)} %dynamic-slice_bitcast_fusion), channel_id=1, source_target_pairs={{0,24},{9,1},{18,10},{27,19},{4,28},{13,5},{22,14},{31,23}} | collective-permute-start | bytes 3932168 | tf_op jit(solution)/shard_map/ppermute | solution.py:179
  306.4 1.4 collective-permute-start.10
  307.8 1.4 collective-permute-start.11
  309.6 6.5 %pad_maximum_fusion.col_ref = bf16[4,10,256,384]{3,2,1,0:T(8,128)(2,1)} fusion(bf16[1,10,256,384]{3,2,1,0:T(8,128)(2,1)} %bitcast.8, bf16[1,10,256,384]{3,2,1,0:T(8,128)(2,1)} %bitcast.7, bf16[1,10,256,384]{3,2,1,0:T(8,128)(2,1)} %bitcast.6, bf16[1,10,256,384]{3,2,1,0:T(8,128)(2,1)S(1)} %fusion.45), kind=kLoop, calls=%fused_computation.3 | loop fusion | flops 11796480 | bytes 15728640 | tf_op jit(solution)/shard_map/stack | solution.py:97
  316.1 31.4 %shard_map.46.refs_0_ = f32[20,1,10,1,256,256]{5,4,3,2,1,0:T(8,128)} custom-call(s32[7]{0:T(128)S(1)} %pad_add_fusion.ids_ref, bf16[2,4,10,256,384]{4,3,2,1,0:T(8,128)(2,1)} %bitcast.129, bf16[4,10,256,384]{3,2,1,0:T(8,128)(2,1)} %pad_maximum_fusion.col_ref, f32[20,1,10,1,256,256]{5,4,3,2,1,0:T(8,128)} %c_ref.3), custom_call_target="tpu_custom_call" | custom-call | tf_op jit(solution)/shard_map/pallas_call | solution.py:192
  347.5 44.7 %shard_map.47.r_ref = f32[20,1,10,1,256,256]{5,4,3,2,1,0:T(8,128)} custom-call(s32[7]{0:T(128)S(1)} %pad_add_fusion.ids_ref, bf16[2,4,10,256,384]{4,3,2,1,0:T(8,128)(2,1)} %bitcast.130, bf16[4,10,256,384]{3,2,1,0:T(8,128)(2,1)} %pad_maximum_fusion.col_ref, f32[20,1,10,1,256,256]{5,4,3,2,1,0:T(8,128)} %c_ref.3, ...), custom_call_target="tpu_custom_call", output_to_operand_aliasing={{}: (4, {})} | custom-call | tf_op jit(solution)/shard_map/pallas_call | solution.py:192
  392.5 30.3 %shard_map.48 = f32[20,1,10,1,256,256]{5,4,3,2,1,0:T(8,128)} custom-call(s32[7]{0:T(128)S(1)} %pad_add_fusion.ids_ref, f32[20,1,10,1,256,256]{5,4,3,2,1,0:T(8,128)} %shard_map.47.r_ref, bf16[20,256,256]{2,1,0:T(8,128)(2,1)S(1)} %copy-done, bf16[10,256,256]{2,1,0:T(8,128)(2,1)S(1)} %add_select_fusion.pcol_ref, ...), custom_call_target="tpu_custom_call", output_to_operand_aliasing={{}: (1, {})} | custom-call | tf_op jit(solution)/shard_map/pallas_call | solution.py:218
  (65 shorter events, 9.7 us)
Async XLA Ops:
  6.5 198.5 %all-gather.3.cloned.1.call-start = ((), (), s32[]{:S(2)}) async-start(), calls=%async_computation.1 | async-start | bytes 17694720 | tf_op jit(solution)/shard_map/all_gather | solution.py:131
  10.7 1.3 copy-start.1
  12.0 1.9 collective-permute-start
  13.9 286.7 %all-reduce.3.cloned.1.call-start = ((), (), s32[]{:S(2)}) async-start(), calls=%async_computation | async-start | bytes 5242880 | tf_op jit(solution)/shard_map/psum | solution.py:17
  15.8 55.3 %collective-permute-start.6 = (bf16[256,384]{1,0:T(8,128)(2,1)}, bf16[256,384]{1,0:T(8,128)(2,1)S(1)}, u32[]{:S(2)}, u32[]{:S(2)}) collective-permute-start(bf16[256,384]{1,0:T(8,128)(2,1)} %get-tuple-element.28), channel_id=1, source_target_pairs={{0,24},{8,0},{16,8},{24,16},{1,25},{9,1},{17,9},{25,17},{2,26},{10... | collective-permute-start | bytes 589832 | tf_op jit(solution)/shard_map/ppermute | solution.py:96
  65.5 17.3 %collective-permute-start.5 = (bf16[256,384]{1,0:T(8,128)(2,1)}, bf16[256,384]{1,0:T(8,128)(2,1)S(1)}, u32[]{:S(2)}, u32[]{:S(2)}) collective-permute-start(bf16[256,384]{1,0:T(8,128)(2,1)} %get-tuple-element.28), channel_id=1, source_target_pairs={{0,16},{8,24},{16,0},{24,8},{1,17},{9,25},{17,1},{25,9},{2,18},{10... | collective-permute-start | bytes 589832 | tf_op jit(solution)/shard_map/ppermute | solution.py:96
  65.5 17.3 %collective-permute-start.4 = (bf16[256,384]{1,0:T(8,128)(2,1)}, bf16[256,384]{1,0:T(8,128)(2,1)S(1)}, u32[]{:S(2)}, u32[]{:S(2)}) collective-permute-start(bf16[256,384]{1,0:T(8,128)(2,1)} %get-tuple-element.28), channel_id=1, source_target_pairs={{0,8},{8,16},{16,24},{24,0},{1,9},{9,17},{17,25},{25,1},{2,10},{10... | collective-permute-start | bytes 589832 | tf_op jit(solution)/shard_map/ppermute | solution.py:96
  67.3 18.9 %collective-permute-start.7 = (f32[256,256]{0,1:T(8,128)S(1)}, f32[256,256]{0,1:T(8,128)}, u32[]{:S(2)}, u32[]{:S(2)}) collective-permute-start(f32[256,256]{0,1:T(8,128)S(1)} %bitcast.132), channel_id=1, source_target_pairs={{0,8},{8,16},{16,24},{24,0},{1,9},{9,17},{17,25},{25,1},{2,10},{10... | collective-permute-start | bytes 786440 | tf_op jit(solution)/shard_map/ppermute | solution.py:96
  70.1 18.4 %collective-permute-start.8 = (f32[256,256]{0,1:T(8,128)S(1)}, f32[256,256]{0,1:T(8,128)}, u32[]{:S(2)}, u32[]{:S(2)}) collective-permute-start(f32[256,256]{0,1:T(8,128)S(1)} %bitcast.133), channel_id=1, source_target_pairs={{0,16},{8,24},{16,0},{24,8},{1,17},{9,25},{17,1},{25,9},{2,18},{10... | collective-permute-start | bytes 786440 | tf_op jit(solution)/shard_map/ppermute | solution.py:96
  71.1 17.4 %collective-permute-start.9 = (f32[256,256]{0,1:T(8,128)S(1)}, f32[256,256]{0,1:T(8,128)}, u32[]{:S(2)}, u32[]{:S(2)}) collective-permute-start(f32[256,256]{0,1:T(8,128)S(1)} %bitcast.134), channel_id=1, source_target_pairs={{0,24},{8,0},{16,8},{24,16},{1,25},{9,1},{17,9},{25,17},{2,26},{10... | collective-permute-start | bytes 786440 | tf_op jit(solution)/shard_map/ppermute | solution.py:96
  82.8 0.7 copy-start.2
  82.8 225.0 %collective-permute-start.3 = (bf16[10,256,384]{2,1,0:T(8,128)(2,1)}, bf16[10,256,384]{2,1,0:T(8,128)(2,1)}, u32[]{:S(2)}, u32[]{:S(2)}) collective-permute-start(bf16[10,256,384]{2,1,0:T(8,128)(2,1)} %copy-done.1), channel_id=1, source_target_pairs={{0,24},{8,0},{16,8},{24,16},{1,25},{9,1},{17,9},{25,17},{2,26},{10... | collective-permute-start | bytes 5898248 | tf_op jit(solution)/shard_map/ppermute | solution.py:96
  82.8 0.7 copy-start.3
  82.8 226.8 %collective-permute-start.2 = (bf16[10,256,384]{2,1,0:T(8,128)(2,1)}, bf16[10,256,384]{2,1,0:T(8,128)(2,1)}, u32[]{:S(2)}, u32[]{:S(2)}) collective-permute-start(bf16[10,256,384]{2,1,0:T(8,128)(2,1)} %copy-done.1), channel_id=1, source_target_pairs={{0,16},{8,24},{16,0},{24,8},{1,17},{9,25},{17,1},{25,9},{2,18},{10... | collective-permute-start | bytes 5898248 | tf_op jit(solution)/shard_map/ppermute | solution.py:96
  86.2 223.4 %collective-permute-start.1 = (bf16[10,256,384]{2,1,0:T(8,128)(2,1)}, bf16[10,256,384]{2,1,0:T(8,128)(2,1)}, u32[]{:S(2)}, u32[]{:S(2)}) collective-permute-start(bf16[10,256,384]{2,1,0:T(8,128)(2,1)} %copy-done.1), channel_id=1, source_target_pairs={{0,8},{8,16},{16,24},{24,0},{1,9},{9,17},{17,25},{25,1},{2,10},{10... | collective-permute-start | bytes 5898248 | tf_op jit(solution)/shard_map/ppermute | solution.py:96
  302.0 90.2 %collective-permute-start.12 = (bf16[10,256,256]{2,1,0:T(8,128)(2,1)S(1)}, bf16[10,256,256]{2,1,0:T(8,128)(2,1)S(1)}, u32[]{:S(2)}, u32[]{:S(2)}) collective-permute-start(bf16[10,256,256]{2,1,0:T(8,128)(2,1)S(1)} %dynamic-slice_bitcast_fusion), channel_id=1, source_target_pairs={{0,24},{9,1},{18,10},{27,19},{4,28},{13,5},{22,14},{31,23}} | collective-permute-start | bytes 3932168 | tf_op jit(solution)/shard_map/ppermute | solution.py:179
  306.4 85.8 %collective-permute-start.10 = (bf16[10,256,256]{2,1,0:T(8,128)(2,1)S(1)}, bf16[10,256,256]{2,1,0:T(8,128)(2,1)S(1)}, u32[]{:S(2)}, u32[]{:S(2)}) collective-permute-start(bf16[10,256,256]{2,1,0:T(8,128)(2,1)S(1)} %dynamic-slice_bitcast_fusion), channel_id=1, source_target_pairs={{0,8},{9,17},{18,26},{27,3},{4,12},{13,21},{22,30},{31,7}} | collective-permute-start | bytes 3932168 | tf_op jit(solution)/shard_map/ppermute | solution.py:179
  307.8 84.4 %collective-permute-start.11 = (bf16[10,256,256]{2,1,0:T(8,128)(2,1)S(1)}, bf16[10,256,256]{2,1,0:T(8,128)(2,1)S(1)}, u32[]{:S(2)}, u32[]{:S(2)}) collective-permute-start(bf16[10,256,256]{2,1,0:T(8,128)(2,1)S(1)} %dynamic-slice_bitcast_fusion), channel_id=1, source_target_pairs={{0,16},{9,25},{18,2},{27,11},{4,20},{13,29},{22,6},{31,15}} | collective-permute-start | bytes 3932168 | tf_op jit(solution)/shard_map/ppermute | solution.py:179
  347.5 44.8 %copy-start = (bf16[20,256,256]{2,1,0:T(8,128)(2,1)S(1)}, bf16[20,256,256]{2,1,0:T(8,128)(2,1)}, u32[]{:S(2)}) copy-start(bf16[20,256,256]{2,1,0:T(8,128)(2,1)} %all-reduce.3.cloned.1.call-done.prow_ref) | copy-start | bytes 7864324
Sparse Core Ops, SparseCore 0:
  14.0 190.8 all-gather.2
  233.3 67.3 all-reduce.2

commit v2 on v1

--- a/solution.py
+++ b/solution.py
@@ -142,7 +142,9 @@
         prior, (panel_at // n_row, panel_at // n_col, 0, 0), (1, 1, width, width)
     )[0, 0]
     diag_prior = gather_row(own_diag, n_row)[(row_index - owner_row) % n_row]
-    col_k = gather_row(lax.dynamic_index_in_dim(local_t, panel_at // n_col, 0, keepdims=False), n_row)
+    col_k = gather_row(
+        lax.dynamic_index_in_dim(local_t, panel_at // n_col, 0, keepdims=False), n_row
+    )
     gram_kk = jnp.einsum("pts,pus->tu", col_k, col_k, preferred_element_type=jnp.float32)
     diag_tile = FORGET * diag_prior + gram_kk / samples
     factor = jnp.linalg.cholesky(diag_tile)
@@ -161,7 +163,7 @@
         "atu,vu->atv",
         column_part,
         inverse,
-        precision=lax.Precision.HIGHEST,
+        precision=lax.Precision.HIGH,
         preferred_element_type=jnp.float32,
     )
     solved = jnp.where((row_tiles > panel_at)[:, None, None], solved, jnp.zeros_like(solved))
@@ -185,7 +187,7 @@
     def late_pick(a, ids):
         return late_row(a, ids, n_row, blocks_a)
 
-    half = blocks_a // 2
+    half = (4 * blocks_a) // 5
 
     def refresh_half(offset, rows, prev):
         extra = [] if prev is None else [prev]

time: 431 us -> 429 us (level)
  no operation moved by 1% of the time
where the time goes in v2:
time: 429 us; the launch traced here: 428 us
  waiting for transfers between devices  129 us (30%)
  Pallas kernels  107 us (25%)
  starting transfers between devices  67.9 us (16%)
  other arithmetic  64.6 us (15%)
  matrix products  23.4 us (5%)
  local copies, waits for them, and re-layouts  20.6 us (5%)
  between operations  15.7 us (4%)
    pallas_call x2, Pallas kernels, refresh_half(): pl.pallas_call(functools.partial(refresh_kernel, n_row=n_row, n_col=n_col...  76.4 us
    psum x1, waiting for transfers between devices, from_root(): return lax.psum(block, axis)  67.4 us
    ppermute x9, starting transfers between devices, gather_row(): lax.ppermute(x, 'row', [(q, (q + s) % n_row) for q in range(n_row)])  58.9 us
    all_gather x1, waiting for transfers between devices, step(): row_g = lax.all_gather(piece, 'col', axis=0, tiled=False)  51.9 us
    another operation x6, other arithmetic, step(): factor = jnp.linalg.cholesky(diag_tile)  34 us
    pallas_call x1, Pallas kernels, step(): pl.pallas_call(functools.partial(update_kernel, n_row=n_row, n_col=n_col,...  30.3 us
    another operation x3, other arithmetic, step(): lax.linalg.triangular_solve(factor, jnp.eye(width, dtype=jnp.float32), le...  20.5 us
    dot_general x1, matrix products, step(): jnp.einsum('hdbts,dus->bhtu', row5, col_k_d, preferred_element_type=jnp.f...  12.4 us
  transfers between devices with their start and end apart: 15, of which 5 were waited for; matrix products, arithmetic and copies ran while one was open for 24% of the time, Pallas kernels for 18%

profile of v2, /device:TPU:0, one launch (start us, length us, event | category | flops | bytes accessed | tf_op | source)
XLA Modules:
  0.0 428.1 jit_solution(18437947859944895553)
XLA Ops:
  7.4 2.8 copy.32
  10.7 1.3 copy-done.1
  12.0 1.9 collective-permute-start
  15.8 49.7 %collective-permute-start.6 = (bf16[256,384]{1,0:T(8,128)(2,1)}, bf16[256,384]{1,0:T(8,128)(2,1)S(1)}, u32[]{:S(2)}, u32[]{:S(2)}) collective-permute-start(bf16[256,384]{1,0:T(8,128)(2,1)} %get-tuple-element.28), channel_id=1, source_target_pairs={{0,24},{8,0},{16,8},{24,16},{1,25},{9,1},{17,9},{25,17},{2,26},{10... | collective-permute-start | bytes 589832 | tf_op jit(solution)/shard_map/ppermute | solution.py:96
  66.2 1.0 constant_dynamic-slice_fusion.1
  67.3 2.8 collective-permute-start.7
  71.1 3.3 collective-permute-start.9
  74.4 8.4 %collective-permute-done.5 = bf16[256,384]{1,0:T(8,128)(2,1)S(1)} collective-permute-done((bf16[256,384]{1,0:T(8,128)(2,1)}, bf16[256,384]{1,0:T(8,128)(2,1)S(1)}, u32[]{:S(2)}, u32[]{:S(2)}) %collective-permute-start.5) | collective-permute-done | bytes 196640 | tf_op jit(solution)/shard_map/ppermute | solution.py:96
  83.5 1.1 pad_maximum_fusion.1
  84.6 1.6 gather_fusion
  86.2 2.0 collective-permute-start.1
  88.5 1.8 fusion.11
  90.4 11.7 %cholesky.50 = f32[128,128]{1,0:T(8,128)S(1)} custom-call(f32[128,128]{1,0:T(8,128)S(1)} %cholesky.118), custom_call_target="Cholesky" | custom-call | tf_op jit(solution)/shard_map/jit(cholesky)/cholesky | solution.py:150
  102.2 9.8 %custom-call.14 = f32[1,128,128]{1,2,0:T(8,128)S(1)} custom-call(f32[1,128,128]{2,1,0:T(8,128)S(1)} %get-tuple-element.32), custom_call_target="InvertDiagBlocksLowerTriangular" | custom-call | tf_op jit(solution)/shard_map/jit(cholesky)/cholesky | solution.py:150
  112.5 11.7 %cholesky.105 = f32[128,128]{1,0:T(8,128)S(1)} custom-call(f32[128,128]{1,0:T(8,128)S(1)} %convolution_subtract_fusion.1), custom_call_target="Cholesky" | custom-call | tf_op jit(solution)/shard_map/jit(cholesky)/cholesky | solution.py:150
  126.4 5.3 %while.1 = (s32[]{:T(128)}, f32[256,256]{1,0:T(8,128)S(1)}, s32[2,2]{1,0:T(2,128)S(1)}, f32[2,128,128]{2,1,0:T(8,128)}, s32[]{:T(128)}) while((s32[]{:T(128)}, f32[256,256]{1,0:T(8,128)S(1)}, s32[2,2]{1,0:T(2,128)S(1)}, f32[2,128,128]{2,1,0:T(8,128)}, s32[]{:T(128)}) %tuple.26), condition=%wide.while_cond, body=%wide.while_body.sunk | while | flops 2 | bytes 132205 | solution.py:151
  127.1 2.0 bitcast_dynamic-update-slice_fusion.2
  129.7 2.0 bitcast_dynamic-update-slice_fusion.2
  131.7 20.5 %custom-call.15 = f32[2,128,128]{1,2,0:T(8,128)S(1)} custom-call(f32[2,128,128]{2,1,0:T(8,128)} %get-tuple-element.12), custom_call_target="InvertDiagBlocksLowerTriangular" | custom-call | tf_op jit(solution)/shard_map/triangular_solve | solution.py:151
  153.1 51.9 %all-gather.3.cloned.1.call-done = bf16[80,256,384]{2,1,0:T(8,128)(2,1)} async-done(((bf16[10,256,384]{2,1,0:T(8,128)(2,1)}), bf16[80,256,384]{2,1,0:T(8,128)(2,1)}) %all-gather.3.cloned.1.call-update) | async-done | bytes 15728656 | tf_op jit(solution)/shard_map/all_gather | solution.py:131
  205.0 12.4 %fusion = f32[10,2,256,256]{2,3,0,1:T(8,128)} fusion(bf16[2,4,10,256,384]{4,3,2,1,0:T(8,128)(2,1)} %bitcast.128, bf16[4,256,384]{2,1,0:T(8,128)(2,1)} %gather_fusion, pred[4]{0:T(512)(128)(4,1)S(1)} %get-tuple-element.23), kind=kOutput, calls=%fused_computation.5 | convolution fusion | flops 4028235776 | bytes 21757956 | tf_op jit(solution)/shard_map/hdbts,dus->bhtu/dot_general | solution.py:156
  217.3 5.9 %copy.35 = f32[10,2,256,256]{3,2,1,0:T(8,128)} copy(f32[10,2,256,256]{2,3,0,1:T(8,128)} %fusion) | data formatting | bytes 10485760 | tf_op jit(solution)/shard_map/div | solution.py:160
  223.2 8.0 %fusion.6 = bf16[20,256,256]{2,1,0:T(8,128)(2,1)} fusion(pred[20]{0:T(512)(128)(4,1)S(1)} %add_compare_fusion, pred[]{:T(512)S(6)} %eq.18, f32[20,256,256]{2,1,0:T(8,128)} %bitcast.131, f32[20,1,10,1,256,256]{5,4,3,2,1,0:T(8,128)} %c_ref.3, s32[]{:T(128)S(6)} %select_n.118, f32[128,256]{1,0:T(8,128)S(1)} %fusion.28, f32[128,256]{1,0:T(8,128)S(1)} %fusion.25), kind=kOutput, calls=%fused_computation.12 | convolution fusion | flops 2019885056 | bytes 13369369 | tf_op jit(solution)/shard_map/atu,vu->atv/dot_general | solution.py:162
  231.3 67.4 %all-reduce.3.cloned.1.call-done.prow_ref = bf16[20,256,256]{2,1,0:T(8,128)(2,1)} async-done(((bf16[20,256,256]{2,1,0:T(8,128)(2,1)}), bf16[20,256,256]{2,1,0:T(8,128)(2,1)}) %all-reduce.3.cloned.1.call-update) | async-done | bytes 2621456 | tf_op jit(solution)/shard_map/psum | solution.py:17
  298.7 1.4 dynamic-slice_bitcast_fusion
  300.1 4.4 %collective-permute-start.12 = (bf16[10,256,256]{2,1,0:T(8,128)(2,1)S(1)}, bf16[10,256,256]{2,1,0:T(8,128)(2,1)S(1)}, u32[]{:S(2)}, u32[]{:S(2)}) collective-permute-start(bf16[10,256,256]{2,1,0:T(8,128)(2,1)S(1)} %dynamic-slice_bitcast_fusion), channel_id=1, source_target_pairs={{0,24},{9,1},{18,10},{27,19},{4,28},{13,5},{22,14},{31,23}} | collective-permute-start | bytes 3932168 | tf_op jit(solution)/shard_map/ppermute | solution.py:181
  304.5 1.4 collective-permute-start.10
  305.9 1.4 collective-permute-start.11
  307.7 6.5 %pad_maximum_fusion.col_ref = bf16[4,10,256,384]{3,2,1,0:T(8,128)(2,1)} fusion(bf16[1,10,256,384]{3,2,1,0:T(8,128)(2,1)} %bitcast.8, bf16[1,10,256,384]{3,2,1,0:T(8,128)(2,1)} %bitcast.7, bf16[1,10,256,384]{3,2,1,0:T(8,128)(2,1)} %bitcast.6, bf16[1,10,256,384]{3,2,1,0:T(8,128)(2,1)S(1)} %fusion.45), kind=kLoop, calls=%fused_computation.3 | loop fusion | flops 11796480 | bytes 15728640 | tf_op jit(solution)/shard_map/stack | solution.py:97
  314.2 52.1 %shard_map.46.refs_0_ = f32[20,1,10,1,256,256]{5,4,3,2,1,0:T(8,128)} custom-call(s32[7]{0:T(128)S(1)} %pad_add_fusion.ids_ref, bf16[2,4,10,256,384]{4,3,2,1,0:T(8,128)(2,1)} %bitcast.129, bf16[4,10,256,384]{3,2,1,0:T(8,128)(2,1)} %pad_maximum_fusion.col_ref, f32[20,1,10,1,256,256]{5,4,3,2,1,0:T(8,128)} %c_ref.3), custom_call_target="tpu_custom_call" | custom-call | tf_op jit(solution)/shard_map/pallas_call | solution.py:194
  366.3 24.4 %shard_map.47.r_ref = f32[20,1,10,1,256,256]{5,4,3,2,1,0:T(8,128)} custom-call(s32[7]{0:T(128)S(1)} %pad_add_fusion.ids_ref, bf16[2,4,10,256,384]{4,3,2,1,0:T(8,128)(2,1)} %bitcast.130, bf16[4,10,256,384]{3,2,1,0:T(8,128)(2,1)} %pad_maximum_fusion.col_ref, f32[20,1,10,1,256,256]{5,4,3,2,1,0:T(8,128)} %c_ref.3, ...), custom_call_target="tpu_custom_call", output_to_operand_aliasing={{}: (4, {})} | custom-call | tf_op jit(solution)/shard_map/pallas_call | solution.py:194
  390.9 30.3 %shard_map.48 = f32[20,1,10,1,256,256]{5,4,3,2,1,0:T(8,128)} custom-call(s32[7]{0:T(128)S(1)} %pad_add_fusion.ids_ref, f32[20,1,10,1,256,256]{5,4,3,2,1,0:T(8,128)} %shard_map.47.r_ref, bf16[20,256,256]{2,1,0:T(8,128)(2,1)S(1)} %copy-done, bf16[10,256,256]{2,1,0:T(8,128)(2,1)S(1)} %add_select_fusion.pcol_ref, ...), custom_call_target="tpu_custom_call", output_to_operand_aliasing={{}: (1, {})} | custom-call | tf_op jit(solution)/shard_map/pallas_call | solution.py:220
  (65 shorter events, 9.7 us)
Async XLA Ops:
  6.5 198.5 %all-gather.3.cloned.1.call-start = ((), (), s32[]{:S(2)}) async-start(), calls=%async_computation.1 | async-start | bytes 17694720 | tf_op jit(solution)/shard_map/all_gather | solution.py:131
  10.7 1.3 copy-start.1
  12.0 1.9 collective-permute-start
  13.9 284.8 %all-reduce.3.cloned.1.call-start = ((), (), s32[]{:S(2)}) async-start(), calls=%async_computation | async-start | bytes 5242880 | tf_op jit(solution)/shard_map/psum | solution.py:17
  15.8 55.3 %collective-permute-start.6 = (bf16[256,384]{1,0:T(8,128)(2,1)}, bf16[256,384]{1,0:T(8,128)(2,1)S(1)}, u32[]{:S(2)}, u32[]{:S(2)}) collective-permute-start(bf16[256,384]{1,0:T(8,128)(2,1)} %get-tuple-element.28), channel_id=1, source_target_pairs={{0,24},{8,0},{16,8},{24,16},{1,25},{9,1},{17,9},{25,17},{2,26},{10... | collective-permute-start | bytes 589832 | tf_op jit(solution)/shard_map/ppermute | solution.py:96
  65.5 17.3 %collective-permute-start.5 = (bf16[256,384]{1,0:T(8,128)(2,1)}, bf16[256,384]{1,0:T(8,128)(2,1)S(1)}, u32[]{:S(2)}, u32[]{:S(2)}) collective-permute-start(bf16[256,384]{1,0:T(8,128)(2,1)} %get-tuple-element.28), channel_id=1, source_target_pairs={{0,16},{8,24},{16,0},{24,8},{1,17},{9,25},{17,1},{25,9},{2,18},{10... | collective-permute-start | bytes 589832 | tf_op jit(solution)/shard_map/ppermute | solution.py:96
  65.5 17.3 %collective-permute-start.4 = (bf16[256,384]{1,0:T(8,128)(2,1)}, bf16[256,384]{1,0:T(8,128)(2,1)S(1)}, u32[]{:S(2)}, u32[]{:S(2)}) collective-permute-start(bf16[256,384]{1,0:T(8,128)(2,1)} %get-tuple-element.28), channel_id=1, source_target_pairs={{0,8},{8,16},{16,24},{24,0},{1,9},{9,17},{17,25},{25,1},{2,10},{10... | collective-permute-start | bytes 589832 | tf_op jit(solution)/shard_map/ppermute | solution.py:96
  67.3 18.9 %collective-permute-start.7 = (f32[256,256]{0,1:T(8,128)S(1)}, f32[256,256]{0,1:T(8,128)}, u32[]{:S(2)}, u32[]{:S(2)}) collective-permute-start(f32[256,256]{0,1:T(8,128)S(1)} %bitcast.132), channel_id=1, source_target_pairs={{0,8},{8,16},{16,24},{24,0},{1,9},{9,17},{17,25},{25,1},{2,10},{10... | collective-permute-start | bytes 786440 | tf_op jit(solution)/shard_map/ppermute | solution.py:96
  70.1 18.4 %collective-permute-start.8 = (f32[256,256]{0,1:T(8,128)S(1)}, f32[256,256]{0,1:T(8,128)}, u32[]{:S(2)}, u32[]{:S(2)}) collective-permute-start(f32[256,256]{0,1:T(8,128)S(1)} %bitcast.133), channel_id=1, source_target_pairs={{0,16},{8,24},{16,0},{24,8},{1,17},{9,25},{17,1},{25,9},{2,18},{10... | collective-permute-start | bytes 786440 | tf_op jit(solution)/shard_map/ppermute | solution.py:96
  71.1 17.4 %collective-permute-start.9 = (f32[256,256]{0,1:T(8,128)S(1)}, f32[256,256]{0,1:T(8,128)}, u32[]{:S(2)}, u32[]{:S(2)}) collective-permute-start(f32[256,256]{0,1:T(8,128)S(1)} %bitcast.134), channel_id=1, source_target_pairs={{0,24},{8,0},{16,8},{24,16},{1,25},{9,1},{17,9},{25,17},{2,26},{10... | collective-permute-start | bytes 786440 | tf_op jit(solution)/shard_map/ppermute | solution.py:96
  82.8 0.7 copy-start.2
  82.8 223.1 %collective-permute-start.3 = (bf16[10,256,384]{2,1,0:T(8,128)(2,1)}, bf16[10,256,384]{2,1,0:T(8,128)(2,1)}, u32[]{:S(2)}, u32[]{:S(2)}) collective-permute-start(bf16[10,256,384]{2,1,0:T(8,128)(2,1)} %copy-done.1), channel_id=1, source_target_pairs={{0,24},{8,0},{16,8},{24,16},{1,25},{9,1},{17,9},{25,17},{2,26},{10... | collective-permute-start | bytes 5898248 | tf_op jit(solution)/shard_map/ppermute | solution.py:96
  82.8 0.7 copy-start.3
  82.8 224.9 %collective-permute-start.2 = (bf16[10,256,384]{2,1,0:T(8,128)(2,1)}, bf16[10,256,384]{2,1,0:T(8,128)(2,1)}, u32[]{:S(2)}, u32[]{:S(2)}) collective-permute-start(bf16[10,256,384]{2,1,0:T(8,128)(2,1)} %copy-done.1), channel_id=1, source_target_pairs={{0,16},{8,24},{16,0},{24,8},{1,17},{9,25},{17,1},{25,9},{2,18},{10... | collective-permute-start | bytes 5898248 | tf_op jit(solution)/shard_map/ppermute | solution.py:96
  86.2 221.5 %collective-permute-start.1 = (bf16[10,256,384]{2,1,0:T(8,128)(2,1)}, bf16[10,256,384]{2,1,0:T(8,128)(2,1)}, u32[]{:S(2)}, u32[]{:S(2)}) collective-permute-start(bf16[10,256,384]{2,1,0:T(8,128)(2,1)} %copy-done.1), channel_id=1, source_target_pairs={{0,8},{8,16},{16,24},{24,0},{1,9},{9,17},{17,25},{25,1},{2,10},{10... | collective-permute-start | bytes 5898248 | tf_op jit(solution)/shard_map/ppermute | solution.py:96
  300.1 90.5 %collective-permute-start.12 = (bf16[10,256,256]{2,1,0:T(8,128)(2,1)S(1)}, bf16[10,256,256]{2,1,0:T(8,128)(2,1)S(1)}, u32[]{:S(2)}, u32[]{:S(2)}) collective-permute-start(bf16[10,256,256]{2,1,0:T(8,128)(2,1)S(1)} %dynamic-slice_bitcast_fusion), channel_id=1, source_target_pairs={{0,24},{9,1},{18,10},{27,19},{4,28},{13,5},{22,14},{31,23}} | collective-permute-start | bytes 3932168 | tf_op jit(solution)/shard_map/ppermute | solution.py:181
  304.5 86.1 %collective-permute-start.10 = (bf16[10,256,256]{2,1,0:T(8,128)(2,1)S(1)}, bf16[10,256,256]{2,1,0:T(8,128)(2,1)S(1)}, u32[]{:S(2)}, u32[]{:S(2)}) collective-permute-start(bf16[10,256,256]{2,1,0:T(8,128)(2,1)S(1)} %dynamic-slice_bitcast_fusion), channel_id=1, source_target_pairs={{0,8},{9,17},{18,26},{27,3},{4,12},{13,21},{22,30},{31,7}} | collective-permute-start | bytes 3932168 | tf_op jit(solution)/shard_map/ppermute | solution.py:181
  305.9 84.8 %collective-permute-start.11 = (bf16[10,256,256]{2,1,0:T(8,128)(2,1)S(1)}, bf16[10,256,256]{2,1,0:T(8,128)(2,1)S(1)}, u32[]{:S(2)}, u32[]{:S(2)}) collective-permute-start(bf16[10,256,256]{2,1,0:T(8,128)(2,1)S(1)} %dynamic-slice_bitcast_fusion), channel_id=1, source_target_pairs={{0,16},{9,25},{18,2},{27,11},{4,20},{13,29},{22,6},{31,15}} | collective-permute-start | bytes 3932168 | tf_op jit(solution)/shard_map/ppermute | solution.py:181
  366.3 24.4 %copy-start = (bf16[20,256,256]{2,1,0:T(8,128)(2,1)S(1)}, bf16[20,256,256]{2,1,0:T(8,128)(2,1)}, u32[]{:S(2)}) copy-start(bf16[20,256,256]{2,1,0:T(8,128)(2,1)} %all-reduce.3.cloned.1.call-done.prow_ref) | copy-start | bytes 7864324
Sparse Core Ops, SparseCore 0:
  14.0 190.8 all-gather.2
  231.4 67.3 all-reduce.2
